TPU v7x, 256 devices: a whole 4x4x8 slice. The times are simulated.
256 devices in a mesh: tm: 64 (over z, x, core), wafer: 4 (over y).
Axes of the slice: x: 4, y: 4, z: 8, core: 2. Of those that a mesh axis runs over, the one named last changes fastest.
Arguments:
- timestream: bfloat16 [1024, 262144], P('wafer', 'tm'), may hold values from -6 to 6
- sample_weight: bfloat16 [1024, 262144], P('wafer', 'tm'), may hold values from 0 to 4
- response: float32 [3, 1024], replicated, may hold values from -1 to 1
- band_filter: bfloat16 [256, 256], replicated, may hold values from -0.375 to 0.375
- whiten: bfloat16 [7, 1024, 1024], P(None, ('tm', 'wafer')), as said below
- group_wafer: int32 [64], replicated, may hold values from 0 to 6
- pointing: bfloat16 [1024, 6, 256, 256], P(('tm', 'wafer')), may hold values from -0.15625 to 0.15625
- tile_list: int32 [1024, 6], P(('tm', 'wafer')), may hold values from 0 to 2047, as said below
- tile_home: int32 [2048], replicated, may hold values from 0 to 2047, as said below
- solution: float32 [2048, 3, 256], P('tm'), may hold values from -6 to 6
- direction: float32 [2048, 3, 256], P('tm'), may hold values from -6 to 6
- cg_scalars: float32 [2], replicated, may hold values from 0.5 to 1.5
Outputs:
- solution_next: float32 [2048, 3, 256], P('tm')
- residual_next: float32 [2048, 3, 256], P('tm')
- direction_next: float32 [2048, 3, 256], P('tm')
Inputs may be any that keep to these rules, and one draw needn't show every extreme that they name: `tile_list`: the tiles named in the spans of one device (one index of tm and one of wafer) are all different; among them at most 2 have their row tile_home on one index of tm, and in every draw, for each index of wafer, some index of tm owns exactly 2 tiles named by every device of that wafer index. A permutation: row tile_home[i] of a map holds sky tile i. `whiten`: each whitening matrix is symmetric.
All inputs are finite; a program needn't handle non-finite values.
Results may differ from a plain program's by a relative error of at most 0.0033.
The roundings to bfloat16 on the way count: a program that leaves them out, or rounds other values in their place, can miss the bound.
Values may be sent and summed in bfloat16 or wider, within the bound.
No kernel may reach another device: no remote copies, remote signals or barrier semaphores. Data moves between devices by JAX's collectives and lax.ppermute only.
A program may use at most 128 MiB of HBM per device.

v0:
```python
import jax
import jax.numpy as jnp
from jax import lax
from jax.sharding import PartitionSpec as P


def shards(
    timestream,
    sample_weight,
    response,
    band_filter,
    whiten,
    group_wafer,
    pointing,
    tile_list,
    tile_home,
    solution,
    direction,
    cg_scalars,
):
    precise_mode = lax.Precision.HIGHEST
    tm_count = lax.axis_size("tm")
    tm_index = lax.axis_index("tm")
    step_size = cg_scalars[0]
    blend_weight = cg_scalars[1]
    updated = solution + step_size * direction
    short_map = updated.astype(jnp.bfloat16)
    tiles_own, comp_count, pixel_count = solution.shape
    spans_here, per_span = tile_list.shape
    samples = band_filter.shape[0]
    det_total = whiten.shape[2]
    row_count = spans_here * per_span
    capacity = max(2, (row_count + tm_count - 1) // tm_count)
    tile_ids = tile_list.reshape(row_count)
    home_rows = jnp.take(tile_home, tile_ids, axis=0)
    owners = home_rows // tiles_own
    local_slot = home_rows % tiles_own
    positions = jnp.arange(row_count, dtype=jnp.int32)
    earlier = (owners[:, None] == owners[None, :]) & (positions[None, :] < positions[:, None])
    before_count = jnp.sum(earlier.astype(jnp.int32), axis=1)
    targets = owners * capacity + before_count
    placing = targets[:, None] == jnp.arange(tm_count * capacity, dtype=jnp.int32)[None, :]
    requests = jnp.sum(jnp.where(placing, local_slot[:, None], 0), axis=0)
    requests = requests.reshape(tm_count, capacity)
    asked_slots = lax.all_to_all(requests, "tm", split_axis=0, concat_axis=0, tiled=True)
    served = jnp.take(short_map, asked_slots, axis=0)
    replies, asked_slots = (
        lax.all_to_all(served, "tm", split_axis=0, concat_axis=0, tiled=True),
        asked_slots,
    )
    fetched = jnp.take(
        replies.reshape(tm_count * capacity, comp_count, pixel_count), targets, axis=0
    )
    fetched = fetched.reshape(spans_here, per_span, comp_count, pixel_count)
    signal_parts = jnp.einsum(
        "cktp,ckjp->cjt", pointing, fetched, preferred_element_type=jnp.float32
    )
    wafer_pick = group_wafer[tm_index]
    matrix = lax.dynamic_index_in_dim(
        lax.all_gather(whiten, ("tm", "wafer"), axis=1, tiled=True), wafer_pick, 0, keepdims=False
    )
    columns, column_weights = (
        lax.all_to_all(timestream, "wafer", split_axis=1, concat_axis=0, tiled=True),
        lax.all_to_all(sample_weight, "wafer", split_axis=1, concat_axis=0, tiled=True),
    )
    column_weights = column_weights.astype(jnp.float32).reshape(det_total, spans_here, samples)
    signal = jnp.einsum("jd,cjt->dct", response, signal_parts, precision=precise_mode)
    errors = (
        (columns.astype(jnp.float32).reshape(det_total, spans_here, samples) - signal)
        * column_weights
    ).astype(jnp.bfloat16)
    filtered = jnp.dot(
        errors.reshape(det_total * spans_here, samples),
        band_filter,
        preferred_element_type=jnp.float32,
    )
    filtered = filtered.astype(jnp.bfloat16).reshape(det_total, spans_here * samples)
    whitened = jnp.dot(matrix, filtered, preferred_element_type=jnp.float32).astype(jnp.bfloat16)
    smoothed = lax.dot_general(
        whitened.reshape(det_total * spans_here, samples),
        band_filter,
        (((1,), (1,)), ((), ())),
        preferred_element_type=jnp.float32,
    )
    smoothed = smoothed.astype(jnp.bfloat16).reshape(det_total, spans_here, samples)
    stokes = jnp.einsum(
        "jd,dct->cjt",
        response,
        smoothed.astype(jnp.float32) * column_weights,
        precision=precise_mode,
    )
    stokes_short = stokes.astype(jnp.bfloat16)
    partial_value = jnp.einsum(
        "cjt,cktp->ckjp", stokes_short, pointing, preferred_element_type=jnp.float32
    )
    partial_value = partial_value.reshape(row_count, comp_count * pixel_count)
    outgoing = jnp.dot(placing.astype(jnp.float32).T, partial_value, precision=precise_mode)
    outgoing = outgoing.reshape(tm_count, capacity, comp_count, pixel_count)
    arrived = lax.all_to_all(outgoing, "tm", split_axis=0, concat_axis=0, tiled=True)
    slot_hits = (
        asked_slots.reshape(-1)[None, :] == jnp.arange(tiles_own, dtype=jnp.int32)[:, None]
    ).astype(jnp.float32)
    owned_sum = jnp.dot(
        slot_hits,
        arrived.reshape(tm_count * capacity, comp_count * pixel_count),
        precision=precise_mode,
    )
    owned_sum = owned_sum.reshape(tiles_own, comp_count, pixel_count)
    summed = lax.psum(owned_sum, "wafer")
    residual_next = summed * float(det_total) ** (-0.5)
    direction_next = residual_next + blend_weight * direction
    return (updated, residual_next, direction_next)


def solution(mesh):
    in_specs = (
        P("wafer", "tm"),
        P("wafer", "tm"),
        P(),
        P(),
        P(None, ("tm", "wafer"), None),
        P(),
        P(("tm", "wafer"), None, None, None),
        P(("tm", "wafer"), None),
        P(),
        P("tm", None, None),
        P("tm", None, None),
        P(),
    )
    out_specs = (P("tm", None, None), P("tm", None, None), P("tm", None, None))
    return jax.shard_map(shards, mesh=mesh, in_specs=in_specs, out_specs=out_specs, check_vma=False)
```

profile of v0, /device:TPU:2, one launch (start us, length us, event | category | flops | bytes accessed | tf_op | source)
XLA Modules:
  0.0 281.9 jit_solution(5731134282750877064)
XLA Ops:
  12.9 12.0 %all-to-all-start = ((s32[64,1,2]{2,1,0:T(1,128)}), s32[64,1,2]{2,1,0:T(1,128)S(1)}, u32[]{:S(2)}, u32[]{:S(2)}) async-start(s32[64,1,2]{2,1,0:T(1,128)} %bitcast.2), calls=%async_computation | async-start | bytes 65536 | tf_op jit(solution)/shard_map/all_to_all | solution.py:45
  28.7 4.8 %all-to-all-done = s32[64,1,2]{2,1,0:T(1,128)S(1)} async-done(((s32[64,1,2]{2,1,0:T(1,128)}), s32[64,1,2]{2,1,0:T(1,128)S(1)}, u32[]{:S(2)}, u32[]{:S(2)}) %all-to-all-start) | async-done | bytes 544 | tf_op jit(solution)/shard_map/all_to_all | solution.py:45
  35.9 5.5 %all-to-all-start.2 = ((bf16[64,2,3,256]{3,1,2,0:T(2,128)(2,1)}), bf16[64,2,3,256]{3,1,2,0:T(2,128)(2,1)S(1)}, u32[]{:S(2)}, u32[]{:S(2)}) async-start(bf16[64,2,3,256]{3,1,2,0:T(2,128)(2,1)} %broadcast_select_fusion), calls=%async_computation.2 | async-start | bytes 393216 | tf_op jit(solution)/shard_map/all_to_all | solution.py:48
  45.5 7.3 %all-to-all-done.2 = bf16[64,2,3,256]{3,1,2,0:T(2,128)(2,1)S(1)} async-done(((bf16[64,2,3,256]{3,1,2,0:T(2,128)(2,1)}), bf16[64,2,3,256]{3,1,2,0:T(2,128)(2,1)S(1)}, u32[]{:S(2)}, u32[]{:S(2)}) %all-to-all-start.2) | async-done | bytes 196640 | tf_op jit(solution)/shard_map/all_to_all | solution.py:48
  52.7 4.5 %all-to-all-start.1 = ((bf16[256,4,1024]{0,2,1:T(8,128)(2,1)}), bf16[256,4,1024]{0,2,1:T(8,128)(2,1)}, u32[]{:S(2)}, u32[]{:S(2)}) async-start(bf16[256,4,1024]{0,2,1:T(8,128)(2,1)} %bitcast.99), calls=%async_computation.1 | async-start | bytes 4194304 | tf_op jit(solution)/shard_map/all_to_all | solution.py:63
  61.3 25.7 %all-to-all-done.1 = bf16[256,4,1024]{0,2,1:T(8,128)(2,1)} async-done(((bf16[256,4,1024]{0,2,1:T(8,128)(2,1)}), bf16[256,4,1024]{0,2,1:T(8,128)(2,1)}, u32[]{:S(2)}, u32[]{:S(2)}) %all-to-all-start.1) | async-done | bytes 2097184 | tf_op jit(solution)/shard_map/all_to_all | solution.py:63
  87.1 4.6 %all-to-all-start.3 = ((bf16[256,4,1024]{0,2,1:T(8,128)(2,1)}), bf16[256,4,1024]{0,2,1:T(8,128)(2,1)}, u32[]{:S(2)}, u32[]{:S(2)}) async-start(bf16[256,4,1024]{0,2,1:T(8,128)(2,1)} %bitcast.98), calls=%async_computation.3 | async-start | bytes 4194304 | tf_op jit(solution)/shard_map/all_to_all | solution.py:64
  99.8 4.8 %copy.114 = f32[4,256,1024]{1,0,2:T(4,128)} copy(f32[4,256,1024]{1,2,0:T(8,128)S(1)} %convert_bitcast_fusion.1) | data formatting | bytes 8388608 | tf_op jit(solution)/shard_map/convert_element_type | solution.py:69
  104.7 5.8 %reshape.326 = f32[1024,4,256]{0,2,1:T(8,128)} reshape(f32[4,256,1024]{1,0,2:T(4,128)} %copy.114) | data formatting | bytes 8388608 | tf_op jit(solution)/shard_map/convert_element_type | solution.py:69
  110.5 20.1 %all-to-all-done.3 = bf16[256,4,1024]{0,2,1:T(8,128)(2,1)} async-done(((bf16[256,4,1024]{0,2,1:T(8,128)(2,1)}), bf16[256,4,1024]{0,2,1:T(8,128)(2,1)}, u32[]{:S(2)}, u32[]{:S(2)}) %all-to-all-start.3) | async-done | bytes 2097184 | tf_op jit(solution)/shard_map/all_to_all | solution.py:64
  132.8 4.7 %copy.124 = f32[4,256,1024]{1,0,2:T(4,128)} copy(f32[4,256,1024]{1,2,0:T(8,128)S(1)} %convert_bitcast_fusion) | data formatting | bytes 8388608 | tf_op jit(solution)/shard_map/convert_element_type | solution.py:66
  137.4 5.9 %reshape.327 = f32[1024,4,256]{0,2,1:T(8,128)} reshape(f32[4,256,1024]{1,0,2:T(4,128)} %copy.124) | data formatting | bytes 8388608 | tf_op jit(solution)/shard_map/convert_element_type | solution.py:66
  143.3 7.2 %fusion.2 = bf16[1024,4,256]{0,2,1:T(8,128)(2,1)} fusion(f32[1024,4,256]{0,2,1:T(8,128)} %reshape.327, f32[1024,4,256]{0,2,1:T(8,128)} %reshape.326, f32[4,3,256]{2,1,0:T(4,128)S(1)} %convolution_bitcast_fusion, f32[3,1024]{1,0:T(4,128)S(1)} %copy-done.4), kind=kOutput, calls=%fused_computation.8 | convolution fusion | flops 40894464 | bytes 10510336 | tf_op jit(solution)/shard_map/jd,cjt->dct/dot_general | solution.py:67
  150.5 4.3 %copy.125 = bf16[1024,4,256]{2,1,0:T(4,128)(2,1)} copy(bf16[1024,4,256]{0,2,1:T(8,128)(2,1)} %fusion.2) | data formatting | bytes 4194304 | tf_op jit(solution)/shard_map/convert_element_type | solution.py:71
  162.5 4.4 %reshape.322 = bf16[1024,1024]{1,0:T(8,128)(2,1)} reshape(bf16[4096,256]{1,0:T(8,128)(2,1)} %convolution_convert_fusion.1) | data formatting | bytes 4194304 | tf_op jit(solution)/shard_map/reshape | solution.py:77
  166.9 7.8 %constant_dynamic-slice_fusion = bf16[1,1024,1024]{2,0,1:T(2,128)(2,1)S(1)} fusion(bf16[7,1024,1024]{2,0,1:T(8,128)(2,1)} %all-gather.2.cloned.1.call-done, s32[]{:T(128)S(6)} %select_n.167), kind=kLoop, calls=%fused_computation.81 | loop fusion | bytes 4194308 | tf_op jit(solution)/shard_map/jit(dynamic_index_in_dim)/dynamic_slice | solution.py:59
  178.4 4.4 %reshape.323 = bf16[4096,256]{1,0:T(8,128)(2,1)} reshape(bf16[1024,1024]{1,0:T(8,128)(2,1)} %fusion.6) | data formatting | bytes 4194304 | tf_op jit(solution)/shard_map/reshape | solution.py:80
  182.8 4.3 %fusion = f32[4096,256]{1,0:T(8,128)} fusion(bf16[4096,256]{1,0:T(8,128)(2,1)} %reshape.323, bf16[256,256]{1,0:T(8,128)(2,1)S(1)} %copy-done.2), kind=kOutput, calls=%fused_computation.4 | convolution fusion | flops 538968064 | bytes 6422528 | tf_op jit(solution)/shard_map/dot_general | solution.py:79
  187.1 5.2 %reshape.328 = f32[1024,4,256]{2,1,0:T(4,128)} reshape(f32[4096,256]{1,0:T(8,128)} %fusion) | data formatting | bytes 8388608 | tf_op jit(solution)/shard_map/convert_element_type | solution.py:89
  192.3 5.2 %copy.126 = f32[1024,4,256]{0,2,1:T(8,128)} copy(f32[1024,4,256]{2,1,0:T(4,128)} %reshape.328) | data formatting | bytes 8388608 | tf_op jit(solution)/shard_map/convert_element_type | solution.py:89
  197.5 7.2 %fusion.10 = bf16[4,256,3,1]{1,2,3,0:T(4,128)(2,1)S(1)} fusion(f32[1024,4,256]{0,2,1:T(8,128)} %copy.126, f32[1024,4,256]{0,2,1:T(8,128)} %reshape.327, f32[3,1024]{1,0:T(4,128)S(1)} %copy-done.4), kind=kOutput, calls=%fused_computation.18 | convolution fusion | flops 38800384 | bytes 8407040 | tf_op jit(solution)/shard_map/jd,dct->cjt/dot_general | solution.py:86
  206.7 6.5 %all-to-all-start.4 = ((f32[64,2,3,256]{3,1,2,0:T(2,128)}), f32[64,2,3,256]{3,1,2,0:T(2,128)S(1)}, u32[]{:S(2)}, u32[]{:S(2)}) async-start(f32[64,2,3,256]{3,1,2,0:T(2,128)} %copy.129), calls=%async_computation.4 | async-start | bytes 786432 | tf_op jit(solution)/shard_map/all_to_all | solution.py:99
  216.7 11.3 %all-to-all-done.4 = f32[64,2,3,256]{3,1,2,0:T(2,128)S(1)} async-done(((f32[64,2,3,256]{3,1,2,0:T(2,128)}), f32[64,2,3,256]{3,1,2,0:T(2,128)S(1)}, u32[]{:S(2)}, u32[]{:S(2)}) %all-to-all-start.4) | async-done | bytes 393248 | tf_op jit(solution)/shard_map/all_to_all | solution.py:99
  232.7 40.0 %all-reduce.2.cloned.1.call-done = f32[32,3,256]{2,0,1:T(8,128)} async-done(((f32[32,3,256]{2,0,1:T(8,128)}), f32[32,3,256]{2,0,1:T(8,128)}) %all-reduce.2.cloned.1.call-update) | async-done | bytes 98320 | tf_op jit(solution)/shard_map/psum | solution.py:109
  (71 shorter events, 52.3 us)
Async XLA Ops:
  7.2 89.8 %copy-start = (bf16[4,6,256,256]{3,2,1,0:T(8,128)(2,1)S(1)}, bf16[4,6,256,256]{3,2,1,0:T(8,128)(2,1)}, u32[]{:S(2)}) copy-start(bf16[4,6,256,256]{3,2,1,0:T(8,128)(2,1)} %param.18) | copy-start | bytes 9437188
  7.2 159.8 %all-gather.2.cloned.1.call-start = ((), (), s32[]{:S(2)}) async-start(), calls=%async_computation.5 | async-start | bytes 16842752 | tf_op jit(solution)/shard_map/all_gather | solution.py:60
  12.9 20.6 %all-to-all-start = ((s32[64,1,2]{2,1,0:T(1,128)}), s32[64,1,2]{2,1,0:T(1,128)S(1)}, u32[]{:S(2)}, u32[]{:S(2)}) async-start(s32[64,1,2]{2,1,0:T(1,128)} %bitcast.2), calls=%async_computation | async-start | bytes 65536 | tf_op jit(solution)/shard_map/all_to_all | solution.py:45
  33.5 0.6 copy-start.3
  35.9 16.9 %all-to-all-start.2 = ((bf16[64,2,3,256]{3,1,2,0:T(2,128)(2,1)}), bf16[64,2,3,256]{3,1,2,0:T(2,128)(2,1)S(1)}, u32[]{:S(2)}, u32[]{:S(2)}) async-start(bf16[64,2,3,256]{3,1,2,0:T(2,128)(2,1)} %broadcast_select_fusion), calls=%async_computation.2 | async-start | bytes 393216 | tf_op jit(solution)/shard_map/all_to_all | solution.py:48
  52.7 34.3 %all-to-all-start.1 = ((bf16[256,4,1024]{0,2,1:T(8,128)(2,1)}), bf16[256,4,1024]{0,2,1:T(8,128)(2,1)}, u32[]{:S(2)}, u32[]{:S(2)}) async-start(bf16[256,4,1024]{0,2,1:T(8,128)(2,1)} %bitcast.99), calls=%async_computation.1 | async-start | bytes 4194304 | tf_op jit(solution)/shard_map/all_to_all | solution.py:63
  61.3 30.6 %copy-start.6 = (s32[64]{0:T(128)S(1)}, s32[64]{0:T(128)}, u32[]{:S(2)}) copy-start(s32[64]{0:T(128)} %param.17) | copy-start | bytes 772
  61.3 33.1 %copy-start.5 = (s32[4,6]{1,0:T(4,128)S(1)}, s32[4,6]{1,0:T(4,128)}, u32[]{:S(2)}) copy-start(s32[4,6]{1,0:T(4,128)} %param.19) | copy-start | bytes 292
  87.1 43.5 %all-to-all-start.3 = ((bf16[256,4,1024]{0,2,1:T(8,128)(2,1)}), bf16[256,4,1024]{0,2,1:T(8,128)(2,1)}, u32[]{:S(2)}, u32[]{:S(2)}) async-start(bf16[256,4,1024]{0,2,1:T(8,128)(2,1)} %bitcast.98), calls=%async_computation.3 | async-start | bytes 4194304 | tf_op jit(solution)/shard_map/all_to_all | solution.py:64
  137.4 5.9 %copy-start.4 = (f32[3,1024]{1,0:T(4,128)S(1)}, f32[3,1024]{1,0:T(4,128)}, u32[]{:S(2)}) copy-start(f32[3,1024]{1,0:T(4,128)} %param.14) | copy-start | bytes 36868
  154.8 4.1 %copy-start.2 = (bf16[256,256]{1,0:T(8,128)(2,1)S(1)}, bf16[256,256]{1,0:T(8,128)(2,1)}, u32[]{:S(2)}) copy-start(bf16[256,256]{1,0:T(8,128)(2,1)} %param.15) | copy-start | bytes 393220
  166.9 7.8 %copy-start.1 = (bf16[1024,1024]{1,0:T(8,128)(2,1)S(1)}, bf16[1024,1024]{1,0:T(8,128)(2,1)}, u32[]{:S(2)}) copy-start(bf16[1024,1024]{1,0:T(8,128)(2,1)} %reshape.322) | copy-start | bytes 6291460
  206.7 21.3 %all-to-all-start.4 = ((f32[64,2,3,256]{3,1,2,0:T(2,128)}), f32[64,2,3,256]{3,1,2,0:T(2,128)S(1)}, u32[]{:S(2)}, u32[]{:S(2)}) async-start(f32[64,2,3,256]{3,1,2,0:T(2,128)} %copy.129), calls=%async_computation.4 | async-start | bytes 786432 | tf_op jit(solution)/shard_map/all_to_all | solution.py:99
  213.2 59.5 %all-reduce.2.cloned.1.call-start = ((), (), s32[]{:S(2)}) async-start(), calls=%async_computation.6 | async-start | bytes 196608 | tf_op jit(solution)/shard_map/psum | solution.py:109
Sparse Core Ops, SparseCore 0:
  12.2 136.2 all-gather.1
  231.3 41.4 all-reduce.1
where the time goes:
time: 284 us; the launch traced here: 282 us
  waiting for transfers between devices  109 us (38%)
  local copies, waits for them, and re-layouts  82.1 us (29%)
  starting transfers between devices  33.1 us (12%)
  matrix products  28.8 us (10%)
  between operations  16.2 us (6%)
  other arithmetic  12.3 us (4%)
    psum x1, waiting for transfers between devices, shards(): summed = lax.psum(owned_sum, 'wafer')  40 us
    all_to_all x1, waiting for transfers between devices, shards(): lax.all_to_all(timestream, 'wafer', split_axis=1, concat_axis=0, tiled=True)  25.7 us
    all_to_all x1, waiting for transfers between devices, shards(): lax.all_to_all(sample_weight, 'wafer', split_axis=1, concat_axis=0, tiled...  20.1 us
    unnamed x19, local copies, waits for them, and re-layouts  12.4 us
    all_to_all x1, starting transfers between devices, shards(): lax.all_to_all(requests, 'tm', split_axis=0, concat_axis=0, tiled=True)  12 us
    all_to_all x1, waiting for transfers between devices, shards(): lax.all_to_all(outgoing, 'tm', split_axis=0, concat_axis=0, tiled=True)  11.3 us
    convert_element_type x2, local copies, waits for them, and re-layouts, shards(): columns.astype(jnp.float32).reshape(det_total, spans_here, samples) - signal  10.7 us
    convert_element_type x2, local copies, waits for them, and re-layouts, shards(): column_weights.astype(jnp.float32).reshape(det_total, spans_here, samples)  10.6 us
  transfers between devices with their start and end apart: 7, of which 6 were waited for; matrix products, arithmetic and copies ran while one was open for 27% of the time, Pallas kernels for 0%

commit v1 on v0

--- a/solution.py
+++ b/solution.py
@@ -60,7 +60,12 @@
         lax.all_gather(whiten, ("tm", "wafer"), axis=1, tiled=True), wafer_pick, 0, keepdims=False
     )
     columns, column_weights = (
-        lax.all_to_all(timestream, "wafer", split_axis=1, concat_axis=0, tiled=True),
+        jnp.concatenate(
+            lax.all_to_all(
+                jnp.stack(jnp.split(timestream, lax.axis_size("wafer"), axis=1)), "wafer", 0, 0
+            ),
+            axis=0,
+        ),
         lax.all_to_all(sample_weight, "wafer", split_axis=1, concat_axis=0, tiled=True),
     )
     column_weights = column_weights.astype(jnp.float32).reshape(det_total, spans_here, samples)

time: 284 us -> 281 us (0.989)
    all_to_all x1, waiting for transfers between devices: 20.1 us -> 26.5 us  [shards(): lax.all_to_all(sample_weight, 'wafer', split_axis=1, concat_axis=0, tiled...]
    all_to_all x1, waiting for transfers between devices: 25.7 us -> 20 us  [shards(): lax.all_to_all(jnp.stack(jnp.split(timestream, lax.axis_size('wafer'), ax...]
    unnamed x19 -> x18, local copies, waits for them, and re-layouts: 12.4 us -> 8.28 us
  transfers between devices with their start and end apart: 7 -> 7, of which waited for: 6 -> 6; matrix products, arithmetic and copies ran while one was open for 27% -> 26% of each run, Pallas kernels for 0% -> 0%
where the time goes in v1:
time: 281 us; the launch traced here: 279 us
  waiting for transfers between devices  110 us (39%)
  local copies, waits for them, and re-layouts  79.5 us (28%)
  starting transfers between devices  33.1 us (12%)
  matrix products  28.8 us (10%)
  between operations  16.2 us (6%)
  other arithmetic  11.7 us (4%)
    psum x1, waiting for transfers between devices, shards(): summed = lax.psum(owned_sum, 'wafer')  39.8 us
    all_to_all x1, waiting for transfers between devices, shards(): lax.all_to_all(sample_weight, 'wafer', split_axis=1, concat_axis=0, tiled...  26.5 us
    all_to_all x1, waiting for transfers between devices, shards(): lax.all_to_all(jnp.stack(jnp.split(timestream, lax.axis_size('wafer'), ax...  20 us
    all_to_all x1, starting transfers between devices, shards(): lax.all_to_all(requests, 'tm', split_axis=0, concat_axis=0, tiled=True)  12 us
    all_to_all x1, waiting for transfers between devices, shards(): lax.all_to_all(outgoing, 'tm', split_axis=0, concat_axis=0, tiled=True)  11.3 us
    convert_element_type x2, local copies, waits for them, and re-layouts, shards(): column_weights.astype(jnp.float32).reshape(det_total, spans_here, samples)  10.7 us
    convert_element_type x2, local copies, waits for them, and re-layouts, shards(): columns.astype(jnp.float32).reshape(det_total, spans_here, samples) - signal  10.6 us
    convert_element_type x2, local copies, waits for them, and re-layouts, shards(): smoothed.astype(jnp.float32) * column_weights  10.5 us
  transfers between devices with their start and end apart: 7, of which 6 were waited for; matrix products, arithmetic and copies ran while one was open for 26% of the time, Pallas kernels for 0%

profile of v1, /device:TPU:2, one launch (start us, length us, event | category | flops | bytes accessed | tf_op | source)
XLA Modules:
  0.0 279.1 jit_solution(15924905309784217733)
XLA Ops:
  12.9 12.0 %all-to-all-start = ((s32[64,1,2]{2,1,0:T(1,128)}), s32[64,1,2]{2,1,0:T(1,128)S(1)}, u32[]{:S(2)}, u32[]{:S(2)}) async-start(s32[64,1,2]{2,1,0:T(1,128)} %bitcast.2), calls=%async_computation | async-start | bytes 65536 | tf_op jit(solution)/shard_map/all_to_all | solution.py:45
  28.6 4.8 %all-to-all-done = s32[64,1,2]{2,1,0:T(1,128)S(1)} async-done(((s32[64,1,2]{2,1,0:T(1,128)}), s32[64,1,2]{2,1,0:T(1,128)S(1)}, u32[]{:S(2)}, u32[]{:S(2)}) %all-to-all-start) | async-done | bytes 544 | tf_op jit(solution)/shard_map/all_to_all | solution.py:45
  35.8 5.5 %all-to-all-start.2 = ((bf16[64,2,3,256]{3,1,2,0:T(2,128)(2,1)}), bf16[64,2,3,256]{3,1,2,0:T(2,128)(2,1)S(1)}, u32[]{:S(2)}, u32[]{:S(2)}) async-start(bf16[64,2,3,256]{3,1,2,0:T(2,128)(2,1)} %broadcast_select_fusion), calls=%async_computation.2 | async-start | bytes 393216 | tf_op jit(solution)/shard_map/all_to_all | solution.py:48
  45.4 7.3 %all-to-all-done.2 = bf16[64,2,3,256]{3,1,2,0:T(2,128)(2,1)S(1)} async-done(((bf16[64,2,3,256]{3,1,2,0:T(2,128)(2,1)}), bf16[64,2,3,256]{3,1,2,0:T(2,128)(2,1)S(1)}, u32[]{:S(2)}, u32[]{:S(2)}) %all-to-all-start.2) | async-done | bytes 196640 | tf_op jit(solution)/shard_map/all_to_all | solution.py:48
  52.8 4.4 %all-to-all-start.3 = ((bf16[256,4,1024]{0,2,1:T(8,128)(2,1)}), bf16[256,4,1024]{0,2,1:T(8,128)(2,1)}, u32[]{:S(2)}, u32[]{:S(2)}) async-start(bf16[256,4,1024]{0,2,1:T(8,128)(2,1)} %bitcast.101), calls=%async_computation.3 | async-start | bytes 4194304 | tf_op jit(solution)/shard_map/all_to_all | solution.py:69
  60.5 26.5 %all-to-all-done.3 = bf16[256,4,1024]{0,2,1:T(8,128)(2,1)} async-done(((bf16[256,4,1024]{0,2,1:T(8,128)(2,1)}), bf16[256,4,1024]{0,2,1:T(8,128)(2,1)}, u32[]{:S(2)}, u32[]{:S(2)}) %all-to-all-start.3) | async-done | bytes 2097184 | tf_op jit(solution)/shard_map/all_to_all | solution.py:69
  87.1 4.7 %all-to-all-start.1 = ((bf16[4,256,1024]{2,1,0:T(8,128)(2,1)}), bf16[4,256,1024]{2,1,0:T(8,128)(2,1)}, u32[]{:S(2)}, u32[]{:S(2)}) async-start(bf16[4,256,1024]{2,1,0:T(8,128)(2,1)} %pad_maximum_fusion), calls=%async_computation.1 | async-start | bytes 4194304 | tf_op jit(solution)/shard_map/all_to_all | solution.py:64
  99.9 4.9 %copy.120 = f32[4,256,1024]{1,0,2:T(4,128)} copy(f32[4,256,1024]{1,2,0:T(8,128)S(1)} %convert_bitcast_fusion) | data formatting | bytes 8388608 | tf_op jit(solution)/shard_map/convert_element_type | solution.py:71
  104.8 5.8 %reshape.325 = f32[1024,4,256]{0,2,1:T(8,128)} reshape(f32[4,256,1024]{1,0,2:T(4,128)} %copy.120) | data formatting | bytes 8388608 | tf_op jit(solution)/shard_map/convert_element_type | solution.py:71
  110.6 20.0 %all-to-all-done.1 = bf16[4,256,1024]{2,1,0:T(8,128)(2,1)} async-done(((bf16[4,256,1024]{2,1,0:T(8,128)(2,1)}), bf16[4,256,1024]{2,1,0:T(8,128)(2,1)}, u32[]{:S(2)}, u32[]{:S(2)}) %all-to-all-start.1) | async-done | bytes 2097184 | tf_op jit(solution)/shard_map/all_to_all | solution.py:64
  130.6 5.3 %reshape.358 = f32[1024,4,256]{2,1,0:T(4,128)} reshape(bf16[4,256,1024]{2,1,0:T(8,128)(2,1)} %all-to-all-done.1) | data formatting | bytes 6291456 | tf_op jit(solution)/shard_map/convert_element_type | solution.py:74
  135.9 5.3 %copy.133 = f32[1024,4,256]{0,2,1:T(8,128)} copy(f32[1024,4,256]{2,1,0:T(4,128)} %reshape.358) | data formatting | bytes 8388608 | tf_op jit(solution)/shard_map/convert_element_type | solution.py:74
  141.2 7.2 %fusion.2 = bf16[1024,4,256]{0,2,1:T(8,128)(2,1)} fusion(f32[1024,4,256]{0,2,1:T(8,128)} %reshape.325, f32[1024,4,256]{0,2,1:T(8,128)} %copy.133, f32[4,3,256]{2,1,0:T(4,128)S(1)} %convolution_bitcast_fusion, f32[3,1024]{1,0:T(4,128)S(1)} %copy-done.4), kind=kOutput, calls=%fused_computation.8 | convolution fusion | flops 40894464 | bytes 10510336 | tf_op jit(solution)/shard_map/jd,cjt->dct/dot_general | solution.py:72
  148.3 4.3 %copy.121 = bf16[1024,4,256]{2,1,0:T(4,128)(2,1)} copy(bf16[1024,4,256]{0,2,1:T(8,128)(2,1)} %fusion.2) | data formatting | bytes 4194304 | tf_op jit(solution)/shard_map/convert_element_type | solution.py:76
  160.3 4.4 %reshape.320 = bf16[1024,1024]{1,0:T(8,128)(2,1)} reshape(bf16[4096,256]{1,0:T(8,128)(2,1)} %convolution_convert_fusion.1) | data formatting | bytes 4194304 | tf_op jit(solution)/shard_map/reshape | solution.py:82
  164.7 7.5 %constant_dynamic-slice_fusion = bf16[1,1024,1024]{2,0,1:T(2,128)(2,1)S(1)} fusion(bf16[7,1024,1024]{2,0,1:T(8,128)(2,1)} %all-gather.2.cloned.1.call-done, s32[]{:T(128)S(6)} %select_n.167), kind=kLoop, calls=%fused_computation.85 | loop fusion | bytes 4194308 | tf_op jit(solution)/shard_map/jit(dynamic_index_in_dim)/dynamic_slice | solution.py:59
  175.9 4.4 %reshape.321 = bf16[4096,256]{1,0:T(8,128)(2,1)} reshape(bf16[1024,1024]{1,0:T(8,128)(2,1)} %fusion.6) | data formatting | bytes 4194304 | tf_op jit(solution)/shard_map/reshape | solution.py:85
  180.3 4.3 %fusion = f32[4096,256]{1,0:T(8,128)} fusion(bf16[4096,256]{1,0:T(8,128)(2,1)} %reshape.321, bf16[256,256]{1,0:T(8,128)(2,1)S(1)} %copy-done.2), kind=kOutput, calls=%fused_computation.4 | convolution fusion | flops 538968064 | bytes 6422528 | tf_op jit(solution)/shard_map/dot_general | solution.py:84
  184.6 5.2 %reshape.326 = f32[1024,4,256]{2,1,0:T(4,128)} reshape(f32[4096,256]{1,0:T(8,128)} %fusion) | data formatting | bytes 8388608 | tf_op jit(solution)/shard_map/convert_element_type | solution.py:94
  189.8 5.3 %copy.122 = f32[1024,4,256]{0,2,1:T(8,128)} copy(f32[1024,4,256]{2,1,0:T(4,128)} %reshape.326) | data formatting | bytes 8388608 | tf_op jit(solution)/shard_map/convert_element_type | solution.py:94
  195.1 7.2 %fusion.10 = bf16[4,256,3,1]{1,2,3,0:T(4,128)(2,1)S(1)} fusion(f32[1024,4,256]{0,2,1:T(8,128)} %copy.122, f32[1024,4,256]{0,2,1:T(8,128)} %reshape.325, f32[3,1024]{1,0:T(4,128)S(1)} %copy-done.4), kind=kOutput, calls=%fused_computation.18 | convolution fusion | flops 38800384 | bytes 8407040 | tf_op jit(solution)/shard_map/jd,dct->cjt/dot_general | solution.py:91
  204.3 6.4 %all-to-all-start.4 = ((f32[64,2,3,256]{3,1,2,0:T(2,128)}), f32[64,2,3,256]{3,1,2,0:T(2,128)S(1)}, u32[]{:S(2)}, u32[]{:S(2)}) async-start(f32[64,2,3,256]{3,1,2,0:T(2,128)} %copy.125), calls=%async_computation.4 | async-start | bytes 786432 | tf_op jit(solution)/shard_map/all_to_all | solution.py:104
  214.3 11.3 %all-to-all-done.4 = f32[64,2,3,256]{3,1,2,0:T(2,128)S(1)} async-done(((f32[64,2,3,256]{3,1,2,0:T(2,128)}), f32[64,2,3,256]{3,1,2,0:T(2,128)S(1)}, u32[]{:S(2)}, u32[]{:S(2)}) %all-to-all-start.4) | async-done | bytes 393248 | tf_op jit(solution)/shard_map/all_to_all | solution.py:104
  230.2 39.8 %all-reduce.2.cloned.1.call-done = f32[32,3,256]{2,0,1:T(8,128)} async-done(((f32[32,3,256]{2,0,1:T(8,128)}), f32[32,3,256]{2,0,1:T(8,128)}) %all-reduce.2.cloned.1.call-update) | async-done | bytes 98320 | tf_op jit(solution)/shard_map/psum | solution.py:114
  (71 shorter events, 49.1 us)
Async XLA Ops:
  7.2 89.8 %copy-start = (bf16[4,6,256,256]{3,2,1,0:T(8,128)(2,1)S(1)}, bf16[4,6,256,256]{3,2,1,0:T(8,128)(2,1)}, u32[]{:S(2)}) copy-start(bf16[4,6,256,256]{3,2,1,0:T(8,128)(2,1)} %param.18) | copy-start | bytes 9437188
  7.2 157.5 %all-gather.2.cloned.1.call-start = ((), (), s32[]{:S(2)}) async-start(), calls=%async_computation.5 | async-start | bytes 16842752 | tf_op jit(solution)/shard_map/all_gather | solution.py:60
  12.9 20.6 %all-to-all-start = ((s32[64,1,2]{2,1,0:T(1,128)}), s32[64,1,2]{2,1,0:T(1,128)S(1)}, u32[]{:S(2)}, u32[]{:S(2)}) async-start(s32[64,1,2]{2,1,0:T(1,128)} %bitcast.2), calls=%async_computation | async-start | bytes 65536 | tf_op jit(solution)/shard_map/all_to_all | solution.py:45
  33.5 0.6 copy-start.3
  35.8 16.9 %all-to-all-start.2 = ((bf16[64,2,3,256]{3,1,2,0:T(2,128)(2,1)}), bf16[64,2,3,256]{3,1,2,0:T(2,128)(2,1)S(1)}, u32[]{:S(2)}, u32[]{:S(2)}) async-start(bf16[64,2,3,256]{3,1,2,0:T(2,128)(2,1)} %broadcast_select_fusion), calls=%async_computation.2 | async-start | bytes 393216 | tf_op jit(solution)/shard_map/all_to_all | solution.py:48
  52.8 34.3 %all-to-all-start.3 = ((bf16[256,4,1024]{0,2,1:T(8,128)(2,1)}), bf16[256,4,1024]{0,2,1:T(8,128)(2,1)}, u32[]{:S(2)}, u32[]{:S(2)}) async-start(bf16[256,4,1024]{0,2,1:T(8,128)(2,1)} %bitcast.101), calls=%async_computation.3 | async-start | bytes 4194304 | tf_op jit(solution)/shard_map/all_to_all | solution.py:69
  60.5 31.4 %copy-start.6 = (s32[64]{0:T(128)S(1)}, s32[64]{0:T(128)}, u32[]{:S(2)}) copy-start(s32[64]{0:T(128)} %param.17) | copy-start | bytes 772
  60.5 34.0 %copy-start.5 = (s32[4,6]{1,0:T(4,128)S(1)}, s32[4,6]{1,0:T(4,128)}, u32[]{:S(2)}) copy-start(s32[4,6]{1,0:T(4,128)} %param.19) | copy-start | bytes 292
  87.1 43.5 %all-to-all-start.1 = ((bf16[4,256,1024]{2,1,0:T(8,128)(2,1)}), bf16[4,256,1024]{2,1,0:T(8,128)(2,1)}, u32[]{:S(2)}, u32[]{:S(2)}) async-start(bf16[4,256,1024]{2,1,0:T(8,128)(2,1)} %pad_maximum_fusion), calls=%async_computation.1 | async-start | bytes 4194304 | tf_op jit(solution)/shard_map/all_to_all | solution.py:64
  135.9 5.3 %copy-start.4 = (f32[3,1024]{1,0:T(4,128)S(1)}, f32[3,1024]{1,0:T(4,128)}, u32[]{:S(2)}) copy-start(f32[3,1024]{1,0:T(4,128)} %param.14) | copy-start | bytes 36868
  152.6 4.0 %copy-start.2 = (bf16[256,256]{1,0:T(8,128)(2,1)S(1)}, bf16[256,256]{1,0:T(8,128)(2,1)}, u32[]{:S(2)}) copy-start(bf16[256,256]{1,0:T(8,128)(2,1)} %param.15) | copy-start | bytes 393220
  164.7 7.5 %copy-start.1 = (bf16[1024,1024]{1,0:T(8,128)(2,1)S(1)}, bf16[1024,1024]{1,0:T(8,128)(2,1)}, u32[]{:S(2)}) copy-start(bf16[1024,1024]{1,0:T(8,128)(2,1)} %reshape.320) | copy-start | bytes 6291460
  204.3 21.2 %all-to-all-start.4 = ((f32[64,2,3,256]{3,1,2,0:T(2,128)}), f32[64,2,3,256]{3,1,2,0:T(2,128)S(1)}, u32[]{:S(2)}, u32[]{:S(2)}) async-start(f32[64,2,3,256]{3,1,2,0:T(2,128)} %copy.125), calls=%async_computation.4 | async-start | bytes 786432 | tf_op jit(solution)/shard_map/all_to_all | solution.py:104
  210.7 59.3 %all-reduce.2.cloned.1.call-start = ((), (), s32[]{:S(2)}) async-start(), calls=%async_computation.6 | async-start | bytes 196608 | tf_op jit(solution)/shard_map/psum | solution.py:114
Sparse Core Ops, SparseCore 0:
  12.2 136.3 all-gather.1
  228.8 41.2 all-reduce.1
